TPU v7x, 256 devices: a whole 4x4x8 slice. The times are simulated.
256 devices in a mesh: req: 32 (over y, z), tp: 8 (over x, core).
Axes of the slice: x: 4, y: 4, z: 8, core: 2. Of those that a mesh axis runs over, the one named last changes fastest.
Arguments:
- tokens: bfloat16 [32768, 1792], P(('req', 'tp')), may hold values from -6 to 6
- norm_gain: float32 [1792], replicated, may hold values from 0.25 to 1.75
- ffn_gain: float32 [1792], replicated, may hold values from 0.25 to 1.75
- mix_weight: bfloat16 [1792, 4, 1792], P('req', None, 'tp'), may hold values from -0.125 to 0.125
- out_weight: bfloat16 [1792, 1792], P('tp', 'req'), may hold values from -0.125 to 0.125
- ffn_weight: bfloat16 [1792, 2, 7168], P('req', None, 'tp'), may hold values from -0.125 to 0.125
- down_weight: bfloat16 [7168, 1792], P('tp', 'req'), may hold values from -0.0625 to 0.0625
- conv_taps: float32 [3, 1792], P(None, 'tp'), may hold values from -3 to 3
- past_cache: bfloat16 [32, 2, 64, 1792], P('req', None, None, 'tp'), may hold values from -210 to 210
- cached_len: int32 [32], P('req'), may hold values from 0 to 8192, as said below
Outputs:
- layer_out: bfloat16 [32768, 1792], P(('req', 'tp'))
- new_cache: bfloat16 [32, 2, 64, 1792], P('req', None, None, 'tp')
Inputs may be any that keep to these rules, and one draw needn't show every extreme that they name: `cached_len`: one request has exactly 8192 cached positions and another fewer than 64.
All inputs are finite; a program needn't handle non-finite values.
Results may differ from a plain program's by a relative error of at most 0.02.
Values may be sent and summed in bfloat16 or wider, within the bound.
No kernel may reach another device: no remote copies, remote signals or barrier semaphores. Data moves between devices by JAX's collectives and lax.ppermute only.
A program may use at most 64 MiB of HBM per device.

v0:
```python
import math
import jax
import jax.numpy as jnp
from jax import lax
from jax.sharding import PartitionSpec as P

HD = 112
WIN = 64


def normed(row_vals, gain):
    floats = row_vals.astype(jnp.float32)
    scaled = floats * lax.rsqrt(jnp.mean(floats * floats, axis=-1, keepdims=True) + 1e-05)
    return (scaled * gain).astype(jnp.bfloat16)


def window_attend(queries, key_rows, value_rows, length, window):
    row_count, head_count, head_size = queries.shape
    block_rows = min(512, row_count)
    score_scale = 1.0 / math.sqrt(head_size)

    def one_block(block_index):
        begin_row = block_index * block_rows
        query_block = lax.dynamic_slice_in_dim(queries, begin_row, block_rows, 0)
        key_block = lax.dynamic_slice_in_dim(key_rows, begin_row, block_rows + window, 0)
        value_block = lax.dynamic_slice_in_dim(value_rows, begin_row, block_rows + window, 0)
        scores = (
            jnp.einsum("qhd,khd->hqk", query_block, key_block, preferred_element_type=jnp.float32)
            * score_scale
        )
        row_ids = begin_row + jnp.arange(block_rows, dtype=jnp.int32)[:, None]
        col_ids = begin_row + jnp.arange(block_rows + window, dtype=jnp.int32)[None, :]
        usable = (col_ids > row_ids) & (col_ids <= row_ids + window) & (col_ids >= window - length)
        scores = jnp.where(usable[None], scores, -1e30)
        row_max = jnp.max(scores, axis=-1, keepdims=True)
        exponent = jnp.exp(scores - row_max)
        weights = (exponent / jnp.sum(exponent, axis=-1, keepdims=True)).astype(jnp.bfloat16)
        return jnp.einsum("hqk,khd->qhd", weights, value_block, preferred_element_type=jnp.float32)

    blocks = lax.map(one_block, jnp.arange(row_count // block_rows, dtype=jnp.int32))
    return blocks.reshape(row_count, head_count, head_size)


def mix_request(projected, cache_rows, length, tap_table, window, head_size):
    row_count, feat_width = (projected.shape[0], projected.shape[2])
    time_order = (length + jnp.arange(window, dtype=jnp.int32)) % window
    earlier = cache_rows[:, time_order]
    key_rows = jnp.concatenate([earlier[0], projected[:, 1]], axis=0)
    value_rows = jnp.concatenate([earlier[1], projected[:, 2]], axis=0)
    head_count = feat_width // head_size
    attended = window_attend(
        projected[:, 0].reshape(row_count, head_count, head_size),
        key_rows.reshape(-1, head_count, head_size),
        value_rows.reshape(-1, head_count, head_size),
        length,
        window,
    ).reshape(row_count, feat_width)
    positions = jnp.arange(window + row_count, dtype=jnp.int32)
    alive_mask = (positions >= window - length)[:, None]
    masked_values = jnp.where(alive_mask, value_rows.astype(jnp.float32), jnp.float32(0.0))
    tap_count = tap_table.shape[0]
    convolved = jnp.zeros((row_count, feat_width), jnp.float32)
    for tap_index in range(tap_count):
        begin_row = window - (tap_count - 1) + tap_index
        convolved = (
            convolved + tap_table[tap_index] * masked_values[begin_row : begin_row + row_count]
        )
    mixed_heads = (attended + projected[:, 3].astype(jnp.float32) * convolved).astype(jnp.bfloat16)
    slot_source = (
        row_count - window + (jnp.arange(window, dtype=jnp.int32) - length - row_count) % window
    )
    renewed = jnp.stack([projected[:, 1], projected[:, 2]])[:, slot_source]
    return (mixed_heads, renewed)


def add_rows(left, shard_piece):
    return jnp.dot(
        left, shard_piece.reshape(shard_piece.shape[0], -1), preferred_element_type=jnp.float32
    )


def local(
    tokens,
    norm_gain,
    ffn_gain,
    mix_weight,
    out_weight,
    ffn_weight,
    down_weight,
    conv_taps,
    past_cache,
    cached_len,
):
    feat_width = mix_weight.shape[2]
    ffn_width = ffn_weight.shape[2]
    normed_all = lax.all_gather(normed(tokens, norm_gain), "tp", axis=0, tiled=True)
    row_total = normed_all.shape[0]
    projected = add_rows(normed_all, lax.all_gather(mix_weight, "req", axis=0, tiled=True))
    projected = projected.astype(jnp.bfloat16).reshape(row_total, 4, feat_width)
    mixed_heads, renewed = mix_request(projected, past_cache[0], cached_len[0], conv_taps, WIN, HD)
    out_columns = lax.all_gather(out_weight, "req", axis=1, tiled=True)
    attn_part = lax.psum_scatter(
        jnp.dot(mixed_heads, out_columns, preferred_element_type=jnp.float32).astype(jnp.bfloat16),
        "tp",
        scatter_dimension=0,
        tiled=True,
    ).astype(jnp.float32)
    residual = (tokens.astype(jnp.float32) + attn_part).astype(jnp.bfloat16)
    ffn_in = lax.all_gather(normed(residual, ffn_gain), "tp", axis=0, tiled=True)
    gate_up = add_rows(ffn_in, lax.all_gather(ffn_weight, "req", axis=0, tiled=True))
    down_columns = lax.all_gather(down_weight, "req", axis=1, tiled=True)
    activated = (jax.nn.silu(gate_up[:, :ffn_width]) * gate_up[:, ffn_width:]).astype(jnp.bfloat16)
    ffn_part = lax.psum_scatter(
        jnp.dot(activated, down_columns, preferred_element_type=jnp.float32).astype(jnp.bfloat16),
        "tp",
        scatter_dimension=0,
        tiled=True,
    ).astype(jnp.float32)
    layer_out = (residual.astype(jnp.float32) + ffn_part).astype(jnp.bfloat16)
    return (layer_out, renewed[None])


def solution(mesh):
    in_specs = (
        P(("req", "tp"), None),
        P(),
        P(),
        P("req", None, "tp"),
        P("tp", "req"),
        P("req", None, "tp"),
        P("tp", "req"),
        P(None, "tp"),
        P("req", None, None, "tp"),
        P("req"),
    )
    out_specs = (P(("req", "tp"), None), P("req", None, None, "tp"))
    return jax.shard_map(local, mesh=mesh, in_specs=in_specs, out_specs=out_specs, check_vma=False)
```

profile of v0, /device:TPU:8, one launch (start us, length us, event | category | flops | bytes accessed | tf_op | source)
XLA Modules:
  0.0 476.0 jit_solution(1445607899470987340)
XLA Ops:
  7.2 0.0 all-gather.8.cloned.1.call-start
  7.2 0.7 all-gather.8.cloned.1.call-update
  7.9 0.0 all-gather.6.cloned.1.call-start
  8.0 1.2 fusion.43
  9.2 2.0 fusion.45
  11.1 0.0 all-gather.6.cloned.1.call-update
  11.1 0.0 reduce-scatter.3.cloned.1.call-start
  11.9 0.9 copy.55
  12.8 0.7 gather_fusion
  13.5 0.1 fusion.70
  13.6 0.1 copy.45
  13.7 0.1 copy.46
  13.9 53.0 %all_gather.20 = bf16[224,1792]{0,1:T(8,128)(2,1)S(1)} all-gather(bf16[224,56]{0,1:T(8,128)(2,1)} %param.16), channel_id=1, replica_groups=mesh['req'=32,'tp'=8] {'req'}, dimensions={1}, use_global_device_ids=true | all-gather | bytes 827904 | tf_op jit(solution)/shard_map/all_gather | solution.py:101
  67.0 26.5 %all-gather.8.cloned.1.call-done = bf16[1792,4,224]{2,1,0:T(4,128)(2,1)} async-done(((bf16[56,4,224]{2,1,0:T(4,128)(2,1)}), bf16[1792,4,224]{2,1,0:T(4,128)(2,1)}) %all-gather.8.cloned.1.call-update) | async-done | bytes 3211280 | tf_op jit(solution)/shard_map/all_gather | solution.py:98
  93.4 6.8 %copy.37 = bf16[1792,4,224]{0,2,1:T(8,128)(2,1)} copy(bf16[1792,4,224]{2,1,0:T(4,128)(2,1)} %all-gather.8.cloned.1.call-done) | data formatting | bytes 6422528 | tf_op jit(solution)/shard_map/all_gather | solution.py:98
  100.2 26.3 %all-gather.6.cloned.1.call-done = bf16[1024,1792]{1,0:T(8,128)(2,1)} async-done(((bf16[128,1792]{1,0:T(8,128)(2,1)}), bf16[1024,1792]{1,0:T(8,128)(2,1)}) %all-gather.6.cloned.1.call-update) | async-done | bytes 3670032 | tf_op jit(solution)/shard_map/all_gather | solution.py:96
  126.4 6.5 %convolution_convert_fusion.2 = bf16[1024,896]{0,1:T(8,128)(2,1)S(1)} fusion(bf16[1024,1792]{1,0:T(8,128)(2,1)} %all-gather.6.cloned.1.call-done, bf16[1792,896]{0,1:T(8,128)(2,1)} %bitcast.62), kind=kOutput, calls=%fused_computation.34 | convolution fusion | flops 3289251840 | bytes 8716288 | tf_op jit(solution)/shard_map/dot_general | solution.py:77
  133.0 0.0 copy-start.2
  133.0 1.2 copy-done.2
  134.2 1.1 slice_bitcast_fusion.2
  135.4 1.0 pad_maximum_fusion.1
  136.4 1.0 pad_maximum_fusion.2
  137.4 32.4 %while.12 = (s32[]{:T(128)}, f32[2,512,2,112]{1,0,3,2:T(2,128)}, s32[2]{0:T(128)S(1)}, bf16[1088,2,112]{0,2,1:T(8,128)(2,1)}, s32[]{:T(128)}, /*index=5*/bf16[10...) while((s32[]{:T(128)}, f32[2,512,2,112]{1,0,3,2:T(2,128)}, ...), condition=%wide.region_4.5_spmd, body=%wide.region_1.4_spmd.sunk | while | flops 402854720 | bytes 4521316 | solution.py:40
  137.4 0.6 dynamic_slice.61
  138.6 0.3 and_and_fusion.2
  139.0 2.2 fusion.90
  141.2 2.7 convolution_bitcast_fusion.2
  143.9 0.5 copy.57
  144.4 9.2 %dynamic_update_slice.7 = f32[2,512,2,112]{1,0,3,2:T(2,128)} dynamic-update-slice(f32[2,512,2,112]{1,0,3,2:T(2,128)} %get-tuple-element.181, f32[1,512,2,112]{1,0,3,2:T(1,128)S(1)} %copy.57, s32[]{:T(128)} %get-tuple-element.180, s32[]{:T(128)} %constant.82.clone.1..sunk, s32[]{:T(128)} %constant.82.clone.1..sunk, s32[]{:T(128)} %constant.82.clone.1..sunk) | dynamic-update-slice | bytes 917508 | tf_op jit(solution)/shard_map/while/body/jit(dynamic_update_index_in_dim)/dynamic_update_slice | solution.py:40
  153.6 0.6 dynamic_slice.61
  154.8 0.3 and_and_fusion.2
  155.2 2.2 fusion.90
  157.4 2.7 convolution_bitcast_fusion.2
  160.1 0.5 copy.57
  160.6 9.2 %dynamic_update_slice.7 = f32[2,512,2,112]{1,0,3,2:T(2,128)} dynamic-update-slice(f32[2,512,2,112]{1,0,3,2:T(2,128)} %get-tuple-element.181, f32[1,512,2,112]{1,0,3,2:T(1,128)S(1)} %copy.57, s32[]{:T(128)} %get-tuple-element.180, s32[]{:T(128)} %constant.82.clone.1..sunk, s32[]{:T(128)} %constant.82.clone.1..sunk, s32[]{:T(128)} %constant.82.clone.1..sunk) | dynamic-update-slice | bytes 917508 | tf_op jit(solution)/shard_map/while/body/jit(dynamic_update_index_in_dim)/dynamic_update_slice | solution.py:40
  169.8 1.3 copy.52
  171.1 0.2 convert_select_fusion
  171.4 5.0 %convolution_convert_fusion.1 = bf16[1024,1792]{1,0:T(8,128)(2,1)} fusion(bf16[224,1792]{0,1:T(8,128)(2,1)S(1)} %all_gather.20, f32[1024,224]{0,1:T(8,128)S(1)} %bitcast.61, f32[1088,224]{0,1:T(8,128)S(1)} %convert_select_fusion, bf16[1024,4,224]{0,2,1:T(8,128)(2,1)} %bitcast.64, f32[224]{0:T(256)S(1)} %bitcast.76, f32[224]{0:T(256)S(1)} %bitcast.77, ...), kind=kOutput, calls=%fused_computation.30 | convolution fusion | flops 825982976 | bytes 8719360 | tf_op jit(solution)/shard_map/dot_general | solution.py:103
  176.4 0.0 reduce-scatter.3.cloned.1.call-update
  176.4 0.0 all-gather.12.cloned.1.call-start
  176.4 0.5 all-gather.12.cloned.1.call-update
  177.0 0.0 all-gather.10.cloned.1.call-start
  177.0 38.8 %reduce-scatter.3.cloned.1.call-done = bf16[128,1792]{1,0:T(8,128)(2,1)} async-done(((bf16[1024,1792]{1,0:T(8,128)(2,1)}), bf16[128,1792]{1,0:T(8,128)(2,1)}) %reduce-scatter.3.cloned.1.call-update) | async-done | bytes 458768 | tf_op jit(solution)/shard_map/reduce_scatter | solution.py:102
  215.8 0.0 copy-done
  215.8 1.3 fusion.47
  217.1 2.0 fusion.49
  219.0 0.0 all-gather.10.cloned.1.call-update
  219.1 0.0 all-gather.14.cloned.1.call-start
  219.1 0.5 all-gather.14.cloned.1.call-update
  219.6 0.2 reduce-scatter.5.cloned.1.call-start
  219.9 85.2 %all-gather.12.cloned.1.call-done = bf16[1792,2,896]{2,1,0:T(2,128)(2,1)} async-done(((bf16[56,2,896]{2,1,0:T(2,128)(2,1)}), bf16[1792,2,896]{2,1,0:T(2,128)(2,1)}) %all-gather.12.cloned.1.call-update) | async-done | bytes 6422544 | tf_op jit(solution)/shard_map/all_gather | solution.py:110
  305.1 6.8 %copy.53 = bf16[224,8,2,896]{3,1,2,0:T(8,128)(2,1)} copy(bf16[224,8,2,896]{3,2,1,0:T(2,128)(2,1)} %bitcast.59) | data formatting | bytes 12845056
  311.9 26.2 %all-gather.10.cloned.1.call-done = bf16[1024,1792]{1,0:T(8,128)(2,1)} async-done(((bf16[128,1792]{1,0:T(8,128)(2,1)}), bf16[1024,1792]{1,0:T(8,128)(2,1)}) %all-gather.10.cloned.1.call-update) | async-done | bytes 3670032 | tf_op jit(solution)/shard_map/all_gather | solution.py:109
  338.1 12.2 %fusion.72 = f32[1024,1792]{1,0:T(8,128)} fusion(bf16[1024,1792]{1,0:T(8,128)(2,1)} %all-gather.10.cloned.1.call-done, bf16[1792,1792]{1,0:T(8,128)(2,1)} %bitcast.60), kind=kOutput, calls=%fused_computation.90 | convolution fusion | flops 6576668672 | bytes 17432576 | tf_op jit(solution)/shard_map/dot_general | solution.py:77
  350.3 69.0 %all-gather.14.cloned.1.call-done = bf16[896,1792]{0,1:T(8,128)(2,1)} async-done(((bf16[896,56]{0,1:T(8,128)(2,1)}), bf16[896,1792]{0,1:T(8,128)(2,1)}) %all-gather.14.cloned.1.call-update) | async-done | bytes 3211280 | tf_op jit(solution)/shard_map/all_gather | solution.py:111
  419.3 10.4 %convolution_convert_fusion = bf16[1024,1792]{1,0:T(8,128)(2,1)} fusion(bf16[896,1792]{0,1:T(8,128)(2,1)} %all-gather.14.cloned.1.call-done, f32[1024,1792]{1,0:T(8,128)} %fusion.72), kind=kOutput, calls=%fused_computation.29 | convolution fusion | flops 3295674368 | bytes 14221312 | tf_op jit(solution)/shard_map/dot_general | solution.py:114
  429.7 0.0 reduce-scatter.5.cloned.1.call-update
  429.8 0.9 copy.42
  430.6 0.9 copy.43
  431.5 3.4 pad_maximum_fusion
  434.9 1.9 gather_fusion.1
  436.8 0.6 copy.44
  437.5 29.8 %reduce-scatter.5.cloned.1.call-done = bf16[128,1792]{1,0:T(8,128)(2,1)} async-done(((bf16[1024,1792]{1,0:T(8,128)(2,1)}), bf16[128,1792]{1,0:T(8,128)(2,1)}) %reduce-scatter.5.cloned.1.call-update) | async-done | bytes 458768 | tf_op jit(solution)/shard_map/reduce_scatter | solution.py:113
  467.2 2.0 fusion.50
  (22 shorter events, 0.1 us)
Async XLA Ops:
  7.2 59.8 %copy-start.4 = (f32[3,224]{1,0:T(4,128)S(1)}, f32[3,224]{1,0:T(4,128)}, u32[]{:S(2)}) copy-start(f32[3,224]{1,0:T(4,128)} %param.19) | copy-start | bytes 8068
  7.2 86.3 %all-gather.8.cloned.1.call-start = ((), (), s32[]{:S(2)}) async-start(), calls=%async_computation.3 | async-start | bytes 3784704 | tf_op jit(solution)/shard_map/all_gather | solution.py:98
  7.9 118.5 %all-gather.6.cloned.1.call-start = ((), (), s32[]{:S(2)}) async-start(), calls=%async_computation.2 | async-start | bytes 4128768 | tf_op jit(solution)/shard_map/all_gather | solution.py:96
  11.1 204.7 %reduce-scatter.3.cloned.1.call-start = ((), (), s32[]{:S(2)}) async-start(), calls=%async_computation.4 | async-start | bytes 4128768 | tf_op jit(solution)/shard_map/reduce_scatter | solution.py:102
  133.0 1.3 copy-start.2
  176.3 39.5 %copy-start = (bf16[128,1792]{1,0:T(8,128)(2,1)S(1)}, bf16[128,1792]{1,0:T(8,128)(2,1)}, u32[]{:S(2)}) copy-start(bf16[128,1792]{1,0:T(8,128)(2,1)} %param.12) | copy-start | bytes 1376260
  176.3 40.7 %copy-start.3 = (f32[1792]{0:T(1024)S(1)}, f32[1792]{0:T(1024)}, u32[]{:S(2)}) copy-start(f32[1792]{0:T(1024)} %param.14) | copy-start | bytes 21508
  176.4 128.7 %all-gather.12.cloned.1.call-start = ((), (), s32[]{:S(2)}) async-start(), calls=%async_computation.6 | async-start | bytes 6623232 | tf_op jit(solution)/shard_map/all_gather | solution.py:110
  177.0 161.2 %all-gather.10.cloned.1.call-start = ((), (), s32[]{:S(2)}) async-start(), calls=%async_computation.5 | async-start | bytes 4128768 | tf_op jit(solution)/shard_map/all_gather | solution.py:109
  219.1 200.3 %all-gather.14.cloned.1.call-start = ((), (), s32[]{:S(2)}) async-start(), calls=%async_computation.7 | async-start | bytes 3311616 | tf_op jit(solution)/shard_map/all_gather | solution.py:111
  219.6 247.6 %reduce-scatter.5.cloned.1.call-start = ((), (), s32[]{:S(2)}) async-start(), calls=%async_computation.8 | async-start | bytes 4128768 | tf_op jit(solution)/shard_map/reduce_scatter | solution.py:113
  429.7 37.5 %copy-start.1 = (bf16[128,1792]{1,0:T(8,128)(2,1)S(1)}, bf16[128,1792]{1,0:T(8,128)(2,1)}, u32[]{:S(2)}) copy-start(bf16[128,1792]{1,0:T(8,128)(2,1)} %reduce-scatter.3.cloned.1.call-done) | copy-start | bytes 1376260
Sparse Core Ops, SparseCore 0:
  10.6 82.8 all-gather.7
  95.8 30.5 all-gather.5
  176.5 39.2 reduce-scatter.2
  218.3 86.7 all-gather.11
  307.3 30.7 all-gather.9
  340.6 78.6 all-gather.13
  429.9 37.3 reduce-scatter.4
where the time goes:
time: 478 us; the launch traced here: 476 us
  waiting for transfers between devices  304 us (64%)
  blocking collectives  53 us (11%)
  local copies, waits for them, and re-layouts  44.1 us (9%)
  matrix products  44 us (9%)
  between operations  14.9 us (3%)
  other arithmetic  14.8 us (3%)
    all_gather x1, waiting for transfers between devices, local(): lax.all_gather(ffn_weight, 'req', axis=0, tiled=True)  85.2 us
    all_gather x1, waiting for transfers between devices, local(): down_columns = lax.all_gather(down_weight, 'req', axis=1, tiled=True)  69 us
    all_gather x1, blocking collectives, local(): out_columns = lax.all_gather(out_weight, 'req', axis=1, tiled=True)  53 us
    reduce_scatter x1, waiting for transfers between devices, local(): lax.psum_scatter(jnp.dot(mixed_heads, out_columns, preferred_element_type...  38.8 us
    reduce_scatter x1, waiting for transfers between devices, local(): lax.psum_scatter(jnp.dot(activated, down_columns, preferred_element_type=...  29.8 us
    all_gather x1, waiting for transfers between devices, local(): lax.all_gather(mix_weight, 'req', axis=0, tiled=True)  26.5 us
    all_gather x1, waiting for transfers between devices, local(): lax.all_gather(normed(tokens, norm_gain), 'tp', axis=0, tiled=True)  26.3 us
    all_gather x1, waiting for transfers between devices, local(): lax.all_gather(normed(residual, ffn_gain), 'tp', axis=0, tiled=True)  26.2 us
  transfers between devices with their start and end apart: 7, of which 7 were waited for; matrix products, arithmetic and copies ran while one was open for 9% of the time, Pallas kernels for 0%

commit v1 on v0

--- a/solution.py
+++ b/solution.py
@@ -6,6 +6,12 @@
 
 HD = 112
 WIN = 64
+
+
+def in_order(blocks, dim):
+    dims = list(blocks.shape[1:])
+    dims[dim] *= blocks.shape[0]
+    return jnp.moveaxis(blocks, 0, dim).reshape(dims)
 
 
 def normed(row_vals, gain):
@@ -106,7 +112,20 @@
         tiled=True,
     ).astype(jnp.float32)
     residual = (tokens.astype(jnp.float32) + attn_part).astype(jnp.bfloat16)
-    ffn_in = lax.all_gather(normed(residual, ffn_gain), "tp", axis=0, tiled=True)
+    value = normed(residual, ffn_gain)
+    size = lax.axis_size("tp")
+    pairs = [(i, (i + 1) % size) for i in range(size)]
+    back = [(b, a) for a, b in pairs]
+    lower, upper = ([], [])
+    for step in range(size - 1):
+        if step % 2 == 0:
+            lower.append(lax.ppermute(lower[-1] if lower else value, "tp", pairs))
+        else:
+            upper.append(lax.ppermute(upper[-1] if upper else value, "tp", back))
+    blocks_2 = jnp.stack([*lower[::-1], value, *upper])
+    shift = lax.axis_index("tp") - len(lower)
+    blocks_2 = blocks_2[(jnp.arange(size) - shift) % size]
+    ffn_in = in_order(blocks_2, 0)
     gate_up = add_rows(ffn_in, lax.all_gather(ffn_weight, "req", axis=0, tiled=True))
     down_columns = lax.all_gather(down_weight, "req", axis=1, tiled=True)
     activated = (jax.nn.silu(gate_up[:, :ffn_width]) * gate_up[:, ffn_width:]).astype(jnp.bfloat16)

time: 478 us -> 443 us (0.927)
  waiting for transfers between devices: 304 us -> 248 us
  local copies, waits for them, and re-layouts: 44.1 us -> 58 us
  starting transfers between devices: 0.46 us -> 8.15 us
    all_gather x1 -> x0, waiting for transfers between devices: 26.2 us -> none  [local(): lax.all_gather(normed(residual, ffn_gain), 'tp', axis=0, tiled=True)]
    all_gather x1, waiting for transfers between devices: 85.2 us -> 59.1 us  [local(): lax.all_gather(ffn_weight, 'req', axis=0, tiled=True)]
    all_gather x1, waiting for transfers between devices: 69 us -> 44.6 us  [local(): down_columns = lax.all_gather(down_weight, 'req', axis=1, tiled=True)]
    ppermute x0 -> x7, waiting for transfers between devices: none -> 21.5 us  [the longest x4 21.5 us: local(): lower.append(lax.ppermute(lower[-1] if lower else value, 'tp', pairs))]
    unnamed x14 -> x21, local copies, waits for them, and re-layouts: 11 us -> 19.7 us
    ppermute x0 -> x7, starting transfers between devices: none -> 7.73 us  [the longest x3 7.7 us: local(): upper.append(lax.ppermute(upper[-1] if upper else value, 'tp', back))]
  transfers between devices with their start and end apart: 7 -> 13, of which waited for: 7 -> 9; matrix products, arithmetic and copies ran while one was open for 9% -> 13% of each run, Pallas kernels for 0% -> 0%
where the time goes in v1:
time: 443 us; the launch traced here: 441 us
  waiting for transfers between devices  248 us (56%)
  local copies, waits for them, and re-layouts  58 us (13%)
  blocking collectives  53 us (12%)
  matrix products  44 us (10%)
  between operations  14.9 us (3%)
  other arithmetic  14 us (3%)
  starting transfers between devices  8.15 us (2%)
    all_gather x1, waiting for transfers between devices, local(): lax.all_gather(ffn_weight, 'req', axis=0, tiled=True)  59.1 us
    all_gather x1, blocking collectives, local(): out_columns = lax.all_gather(out_weight, 'req', axis=1, tiled=True)  53 us
    all_gather x1, waiting for transfers between devices, local(): down_columns = lax.all_gather(down_weight, 'req', axis=1, tiled=True)  44.6 us
    reduce_scatter x1, waiting for transfers between devices, local(): lax.psum_scatter(jnp.dot(mixed_heads, out_columns, preferred_element_type...  38.8 us
    reduce_scatter x1, waiting for transfers between devices, local(): lax.psum_scatter(jnp.dot(activated, down_columns, preferred_element_type=...  29.8 us
    all_gather x1, waiting for transfers between devices, local(): lax.all_gather(mix_weight, 'req', axis=0, tiled=True)  26.5 us
    all_gather x1, waiting for transfers between devices, local(): lax.all_gather(normed(tokens, norm_gain), 'tp', axis=0, tiled=True)  26.3 us
    ppermute x4, waiting for transfers between devices, local(): lower.append(lax.ppermute(lower[-1] if lower else value, 'tp', pairs))  21.5 us
  transfers between devices with their start and end apart: 13, of which 9 were waited for; matrix products, arithmetic and copies ran while one was open for 13% of the time, Pallas kernels for 0%

profile of v1, /device:TPU:8, one launch (start us, length us, event | category | flops | bytes accessed | tf_op | source)
XLA Modules:
  0.0 441.2 jit_solution(13733670333173644959)
XLA Ops:
  7.2 0.7 all-gather.7.cloned.1.call-update
  8.0 1.2 fusion.43
  9.2 2.0 fusion.45
  11.9 0.9 copy.55
  12.8 0.7 gather_fusion
  13.6 0.1 copy.45
  13.7 0.1 copy.46
  13.9 53.0 %all_gather.17 = bf16[224,1792]{0,1:T(8,128)(2,1)S(1)} all-gather(bf16[224,56]{0,1:T(8,128)(2,1)} %param.16), channel_id=1, replica_groups=mesh['req'=32,'tp'=8] {'req'}, dimensions={1}, use_global_device_ids=true | all-gather | bytes 827904 | tf_op jit(solution)/shard_map/all_gather | solution.py:107
  67.0 26.5 %all-gather.7.cloned.1.call-done = bf16[1792,4,224]{2,1,0:T(4,128)(2,1)} async-done(((bf16[56,4,224]{2,1,0:T(4,128)(2,1)}), bf16[1792,4,224]{2,1,0:T(4,128)(2,1)}) %all-gather.7.cloned.1.call-update) | async-done | bytes 3211280 | tf_op jit(solution)/shard_map/all_gather | solution.py:104
  93.4 6.7 %copy.37 = bf16[1792,4,224]{0,2,1:T(8,128)(2,1)} copy(bf16[1792,4,224]{2,1,0:T(4,128)(2,1)} %all-gather.7.cloned.1.call-done) | data formatting | bytes 6422528 | tf_op jit(solution)/shard_map/all_gather | solution.py:104
  100.2 26.3 %all-gather.5.cloned.1.call-done = bf16[1024,1792]{1,0:T(8,128)(2,1)} async-done(((bf16[128,1792]{1,0:T(8,128)(2,1)}), bf16[1024,1792]{1,0:T(8,128)(2,1)}) %all-gather.5.cloned.1.call-update) | async-done | bytes 3670032 | tf_op jit(solution)/shard_map/all_gather | solution.py:102
  126.4 6.5 %convolution_convert_fusion.2 = bf16[1024,896]{0,1:T(8,128)(2,1)S(1)} fusion(bf16[1024,1792]{1,0:T(8,128)(2,1)} %all-gather.5.cloned.1.call-done, bf16[1792,896]{0,1:T(8,128)(2,1)} %bitcast.82), kind=kOutput, calls=%fused_computation.35 | convolution fusion | flops 3289251840 | bytes 8716288 | tf_op jit(solution)/shard_map/dot_general | solution.py:83
  133.0 1.3 copy-done.2
  134.3 1.0 slice_bitcast_fusion.2
  135.3 1.0 pad_maximum_fusion.1
  136.3 1.0 pad_maximum_fusion.2
  137.3 32.2 %while.12 = (s32[]{:T(128)}, f32[2,512,2,112]{1,0,3,2:T(2,128)}, s32[2]{0:T(128)S(1)}, bf16[1088,2,112]{0,2,1:T(8,128)(2,1)}, s32[]{:T(128)}, /*index=5*/bf16[10...) while((s32[]{:T(128)}, f32[2,512,2,112]{1,0,3,2:T(2,128)}, ...), condition=%wide.region_4.5_spmd, body=%wide.region_1.4_spmd.sunk | while | flops 402854720 | bytes 4521316 | solution.py:46
  137.3 0.6 dynamic_slice.61
  138.5 0.3 and_and_fusion.2
  138.8 2.2 fusion.92
  141.1 2.7 convolution_bitcast_fusion.2
  143.8 0.5 copy.57
  144.3 9.2 %dynamic_update_slice.7 = f32[2,512,2,112]{1,0,3,2:T(2,128)} dynamic-update-slice(f32[2,512,2,112]{1,0,3,2:T(2,128)} %get-tuple-element.181, f32[1,512,2,112]{1,0,3,2:T(1,128)S(1)} %copy.57, s32[]{:T(128)} %get-tuple-element.180, s32[]{:T(128)} %constant.101.clone.1..sunk, s32[]{:T(128)} %constant.101.clone.1..sunk, s32[]{:T(128)} %constant.101.clone.1..sunk) | dynamic-update-slice | bytes 917508 | tf_op jit(solution)/shard_map/while/body/jit(dynamic_update_index_in_dim)/dynamic_update_slice | solution.py:46
  153.5 0.5 dynamic_slice.61
  154.6 0.3 and_and_fusion.2
  155.0 2.2 fusion.92
  157.2 2.7 convolution_bitcast_fusion.2
  159.9 0.5 copy.57
  160.4 9.2 %dynamic_update_slice.7 = f32[2,512,2,112]{1,0,3,2:T(2,128)} dynamic-update-slice(f32[2,512,2,112]{1,0,3,2:T(2,128)} %get-tuple-element.181, f32[1,512,2,112]{1,0,3,2:T(1,128)S(1)} %copy.57, s32[]{:T(128)} %get-tuple-element.180, s32[]{:T(128)} %constant.101.clone.1..sunk, s32[]{:T(128)} %constant.101.clone.1..sunk, s32[]{:T(128)} %constant.101.clone.1..sunk) | dynamic-update-slice | bytes 917508 | tf_op jit(solution)/shard_map/while/body/jit(dynamic_update_index_in_dim)/dynamic_update_slice | solution.py:46
  169.5 1.3 copy.52
  170.9 0.2 convert_select_fusion
  171.1 5.0 %convolution_convert_fusion.1 = bf16[1024,1792]{1,0:T(8,128)(2,1)} fusion(bf16[224,1792]{0,1:T(8,128)(2,1)S(1)} %all_gather.17, f32[1024,224]{0,1:T(8,128)S(1)} %bitcast.81, f32[1088,224]{0,1:T(8,128)S(1)} %convert_select_fusion, bf16[1024,4,224]{0,2,1:T(8,128)(2,1)} %bitcast.84, f32[224]{0:T(256)S(1)} %bitcast.95, f32[224]{0:T(256)S(1)} %bitcast.96, ...), kind=kOutput, calls=%fused_computation.31 | convolution fusion | flops 825982976 | bytes 8719360 | tf_op jit(solution)/shard_map/dot_general | solution.py:109
  176.2 0.5 all-gather.9.cloned.1.call-update
  176.8 38.8 %reduce-scatter.3.cloned.1.call-done = bf16[128,1792]{1,0:T(8,128)(2,1)} async-done(((bf16[1024,1792]{1,0:T(8,128)(2,1)}), bf16[128,1792]{1,0:T(8,128)(2,1)}) %reduce-scatter.3.cloned.1.call-update) | async-done | bytes 458768 | tf_op jit(solution)/shard_map/reduce_scatter | solution.py:108
  215.6 1.3 fusion.47
  216.9 1.2 fusion.49
  218.1 9.1 %collective-permute-done = bf16[128,1792]{1,0:T(8,128)(2,1)S(1)} collective-permute-done((bf16[128,1792]{1,0:T(8,128)(2,1)S(1)}, bf16[128,1792]{1,0:T(8,128)(2,1)S(1)}, u32[]{:S(2)}, u32[]{:S(2)}) %collective-permute-start) | collective-permute-done | bytes 458784 | tf_op jit(solution)/shard_map/ppermute | solution.py:122
  227.2 3.0 collective-permute-start.4
  230.2 6.2 %collective-permute-done.1 = bf16[128,1792]{1,0:T(8,128)(2,1)S(1)} collective-permute-done((bf16[128,1792]{1,0:T(8,128)(2,1)S(1)}, bf16[128,1792]{1,0:T(8,128)(2,1)S(1)}, u32[]{:S(2)}, u32[]{:S(2)}) %collective-permute-start.1) | collective-permute-done | bytes 458784 | tf_op jit(solution)/shard_map/ppermute | solution.py:122
  236.3 3.0 collective-permute-start.5
  239.3 6.3 %collective-permute-done.2 = bf16[128,1792]{1,0:T(8,128)(2,1)} collective-permute-done((bf16[128,1792]{1,0:T(8,128)(2,1)S(1)}, bf16[128,1792]{1,0:T(8,128)(2,1)}, u32[]{:S(2)}, u32[]{:S(2)}) %collective-permute-start.2) | collective-permute-done | bytes 458784 | tf_op jit(solution)/shard_map/ppermute | solution.py:122
  245.6 0.2 reduce-scatter.5.cloned.1.call-start
  245.9 59.1 %all-gather.9.cloned.1.call-done = bf16[1792,2,896]{2,1,0:T(2,128)(2,1)} async-done(((bf16[56,2,896]{2,1,0:T(2,128)(2,1)}), bf16[1792,2,896]{2,1,0:T(2,128)(2,1)}) %all-gather.9.cloned.1.call-update) | async-done | bytes 6422544 | tf_op jit(solution)/shard_map/all_gather | solution.py:129
  304.9 6.8 %copy.53 = bf16[224,8,2,896]{3,1,2,0:T(8,128)(2,1)} copy(bf16[224,8,2,896]{3,2,1,0:T(2,128)(2,1)} %bitcast.78) | data formatting | bytes 12845056
  311.7 1.8 collective-permute-start.6
  313.5 1.8 bitcast_dynamic-update-slice_fusion.7
  315.4 1.8 bitcast_dynamic-update-slice_fusion.6
  317.2 0.8 bitcast_dynamic-update-slice_fusion.5
  318.0 0.8 bitcast_dynamic-update-slice_fusion.4
  318.8 0.8 bitcast_dynamic-update-slice_fusion.3
  319.6 0.8 bitcast_dynamic-update-slice_fusion.2
  320.4 1.8 bitcast_dynamic-update-slice_fusion.1
  322.2 0.8 bitcast_dynamic-update-slice_fusion
  323.0 4.6 %gather_fusion.1 = bf16[8,128,1792]{2,1,0:T(8,128)(2,1)} fusion(bf16[8,128,1792]{2,1,0:T(8,128)(2,1)} %bitcast_dynamic-update-slice_fusion, s32[1024]{0:T(1024)S(1)} %pad_clamp_fusion.1), kind=kCustom, calls=%fused_computation.1 | custom fusion | bytes 7340064 | tf_op jit(solution)/shard_map/gather | solution.py:127
  327.7 12.2 %fusion.74 = f32[1024,1792]{1,0:T(8,128)} fusion(bf16[1024,1792]{1,0:T(8,128)(2,1)} %bitcast.80, bf16[1792,1792]{1,0:T(8,128)(2,1)} %bitcast.79), kind=kOutput, calls=%fused_computation.106 | convolution fusion | flops 6576668672 | bytes 17432576 | tf_op jit(solution)/shard_map/dot_general | solution.py:83
  339.9 44.6 %all-gather.11.cloned.1.call-done = bf16[896,1792]{0,1:T(8,128)(2,1)} async-done(((bf16[896,56]{0,1:T(8,128)(2,1)}), bf16[896,1792]{0,1:T(8,128)(2,1)}) %all-gather.11.cloned.1.call-update) | async-done | bytes 3211280 | tf_op jit(solution)/shard_map/all_gather | solution.py:130
  384.5 10.4 %convolution_convert_fusion = bf16[1024,1792]{1,0:T(8,128)(2,1)} fusion(bf16[896,1792]{0,1:T(8,128)(2,1)} %all-gather.11.cloned.1.call-done, f32[1024,1792]{1,0:T(8,128)} %fusion.74), kind=kOutput, calls=%fused_computation.30 | convolution fusion | flops 3295674368 | bytes 14221312 | tf_op jit(solution)/shard_map/dot_general | solution.py:133
  394.9 0.9 copy.42
  395.7 0.9 copy.43
  396.6 3.4 pad_maximum_fusion
  400.0 1.9 gather_fusion.2
  402.0 0.6 copy.44
  402.6 29.8 %reduce-scatter.5.cloned.1.call-done = bf16[128,1792]{1,0:T(8,128)(2,1)} async-done(((bf16[1024,1792]{1,0:T(8,128)(2,1)}), bf16[128,1792]{1,0:T(8,128)(2,1)}) %reduce-scatter.5.cloned.1.call-update) | async-done | bytes 458768 | tf_op jit(solution)/shard_map/reduce_scatter | solution.py:132
  432.4 2.0 fusion.50
  (44 shorter events, 0.5 us)
Async XLA Ops:
  7.2 59.8 %copy-start.4 = (f32[3,224]{1,0:T(4,128)S(1)}, f32[3,224]{1,0:T(4,128)}, u32[]{:S(2)}) copy-start(f32[3,224]{1,0:T(4,128)} %param.19) | copy-start | bytes 8068
  7.2 86.3 %all-gather.7.cloned.1.call-start = ((), (), s32[]{:S(2)}) async-start(), calls=%async_computation.3 | async-start | bytes 3784704 | tf_op jit(solution)/shard_map/all_gather | solution.py:104
  7.9 118.5 %all-gather.5.cloned.1.call-start = ((), (), s32[]{:S(2)}) async-start(), calls=%async_computation.2 | async-start | bytes 4128768 | tf_op jit(solution)/shard_map/all_gather | solution.py:102
  11.1 204.5 %reduce-scatter.3.cloned.1.call-start = ((), (), s32[]{:S(2)}) async-start(), calls=%async_computation.4 | async-start | bytes 4128768 | tf_op jit(solution)/shard_map/reduce_scatter | solution.py:108
  133.0 1.3 copy-start.2
  171.1 44.5 %copy-start = (bf16[128,1792]{1,0:T(8,128)(2,1)S(1)}, bf16[128,1792]{1,0:T(8,128)(2,1)}, u32[]{:S(2)}) copy-start(bf16[128,1792]{1,0:T(8,128)(2,1)} %param.12) | copy-start | bytes 1376260
  176.2 40.7 %copy-start.3 = (f32[1792]{0:T(1024)S(1)}, f32[1792]{0:T(1024)}, u32[]{:S(2)}) copy-start(f32[1792]{0:T(1024)} %param.14) | copy-start | bytes 21508
  176.2 128.7 %all-gather.9.cloned.1.call-start = ((), (), s32[]{:S(2)}) async-start(), calls=%async_computation.5 | async-start | bytes 6623232 | tf_op jit(solution)/shard_map/all_gather | solution.py:129
  176.8 207.7 %all-gather.11.cloned.1.call-start = ((), (), s32[]{:S(2)}) async-start(), calls=%async_computation.6 | async-start | bytes 3311616 | tf_op jit(solution)/shard_map/all_gather | solution.py:130
  218.1 9.1 %collective-permute-start = (bf16[128,1792]{1,0:T(8,128)(2,1)S(1)}, bf16[128,1792]{1,0:T(8,128)(2,1)S(1)}, u32[]{:S(2)}, u32[]{:S(2)}) collective-permute-start(bf16[128,1792]{1,0:T(8,128)(2,1)S(1)} %fusion.49), channel_id=1, source_target_pairs={{0,1},{1,2},{2,3},{3,4},{4,5},{5,6},{6,7},{7,0},{8,9},{9,10},{10,1... | collective-permute-start | bytes 1376264 | tf_op jit(solution)/shard_map/ppermute | solution.py:122
  227.2 9.1 %collective-permute-start.1 = (bf16[128,1792]{1,0:T(8,128)(2,1)S(1)}, bf16[128,1792]{1,0:T(8,128)(2,1)S(1)}, u32[]{:S(2)}, u32[]{:S(2)}) collective-permute-start(bf16[128,1792]{1,0:T(8,128)(2,1)S(1)} %collective-permute-done), channel_id=1, source_target_pairs={{0,1},{1,2},{2,3},{3,4},{4,5},{5,6},{6,7},{7,0},{8,9},{9,10},{10,1... | collective-permute-start | bytes 1376264 | tf_op jit(solution)/shard_map/ppermute | solution.py:122
  227.2 9.1 %collective-permute-start.4 = (bf16[128,1792]{1,0:T(8,128)(2,1)S(1)}, bf16[128,1792]{1,0:T(8,128)(2,1)S(1)}, u32[]{:S(2)}, u32[]{:S(2)}) collective-permute-start(bf16[128,1792]{1,0:T(8,128)(2,1)S(1)} %fusion.49), channel_id=1, source_target_pairs={{1,0},{2,1},{3,2},{4,3},{5,4},{6,5},{7,6},{0,7},{9,8},{10,9},{11,1... | collective-permute-start | bytes 1376264 | tf_op jit(solution)/shard_map/ppermute | solution.py:124
  236.3 9.2 %collective-permute-start.2 = (bf16[128,1792]{1,0:T(8,128)(2,1)S(1)}, bf16[128,1792]{1,0:T(8,128)(2,1)}, u32[]{:S(2)}, u32[]{:S(2)}) collective-permute-start(bf16[128,1792]{1,0:T(8,128)(2,1)S(1)} %collective-permute-done.1), channel_id=1, source_target_pairs={{0,1},{1,2},{2,3},{3,4},{4,5},{5,6},{6,7},{7,0},{8,9},{9,10},{10,1... | collective-permute-start | bytes 1376264 | tf_op jit(solution)/shard_map/ppermute | solution.py:122
  236.3 75.4 %collective-permute-start.5 = (bf16[128,1792]{1,0:T(8,128)(2,1)S(1)}, bf16[128,1792]{1,0:T(8,128)(2,1)}, u32[]{:S(2)}, u32[]{:S(2)}) collective-permute-start(bf16[128,1792]{1,0:T(8,128)(2,1)S(1)} %collective-permute-done.4), channel_id=1, source_target_pairs={{1,0},{2,1},{3,2},{4,3},{5,4},{6,5},{7,6},{0,7},{9,8},{10,9},{11,1... | collective-permute-start | bytes 1376264 | tf_op jit(solution)/shard_map/ppermute | solution.py:124
  245.6 68.0 %collective-permute-start.3 = (bf16[128,1792]{1,0:T(8,128)(2,1)}, bf16[128,1792]{1,0:T(8,128)(2,1)}, u32[]{:S(2)}, u32[]{:S(2)}) collective-permute-start(bf16[128,1792]{1,0:T(8,128)(2,1)} %collective-permute-done.2), channel_id=1, source_target_pairs={{0,1},{1,2},{2,3},{3,4},{4,5},{5,6},{6,7},{7,0},{8,9},{9,10},{10,1... | collective-permute-start | bytes 1376264 | tf_op jit(solution)/shard_map/ppermute | solution.py:122
  245.6 186.8 %reduce-scatter.5.cloned.1.call-start = ((), (), s32[]{:S(2)}) async-start(), calls=%async_computation.7 | async-start | bytes 4128768 | tf_op jit(solution)/shard_map/reduce_scatter | solution.py:132
  311.7 10.5 %collective-permute-start.6 = (bf16[128,1792]{1,0:T(8,128)(2,1)}, bf16[128,1792]{1,0:T(8,128)(2,1)S(1)}, u32[]{:S(2)}, u32[]{:S(2)}) collective-permute-start(bf16[128,1792]{1,0:T(8,128)(2,1)} %collective-permute-done.5), channel_id=1, source_target_pairs={{1,0},{2,1},{3,2},{4,3},{5,4},{6,5},{7,6},{0,7},{9,8},{10,9},{11,1... | collective-permute-start | bytes 1376264 | tf_op jit(solution)/shard_map/ppermute | solution.py:124
  394.9 37.6 %copy-start.1 = (bf16[128,1792]{1,0:T(8,128)(2,1)S(1)}, bf16[128,1792]{1,0:T(8,128)(2,1)}, u32[]{:S(2)}) copy-start(bf16[128,1792]{1,0:T(8,128)(2,1)} %reduce-scatter.3.cloned.1.call-done) | copy-start | bytes 1376260
Sparse Core Ops, SparseCore 0:
  10.6 82.8 all-gather.6
  95.8 30.5 all-gather.4
  176.3 39.2 reduce-scatter.2
  218.1 86.7 all-gather.8
  307.4 77.0 all-gather.10
  395.0 37.4 reduce-scatter.4
